TPU v7x, 32 devices: a whole 2x2x4 slice. The times are simulated.
32 devices in a mesh: seq: 16 (over z, x, core), batch: 2 (over y).
Axes of the slice: x: 2, y: 2, z: 4, core: 2. Of those that a mesh axis runs over, the one named last changes fastest.
Arguments:
- activations: bfloat16 [2, 8192, 1536], P('batch', 'seq'), may hold values from -60 to 60
- cotangent: bfloat16 [2, 8192, 1536], P('batch', 'seq'), may hold values from -6 to 6
- contig_lengths: int32 [2, 4], P('batch'), may hold values from 1 to 4096, 8192 in all within a row
- gain_input: float32 [1536], replicated, may hold values from 0.1 to 1.9
- tap_weights: bfloat16 [3, 1536, 768], replicated, may hold values from -0.09375 to 0.09375
- gain_middle: float32 [768], replicated, may hold values from 0.1 to 1.9
- point_weights: bfloat16 [768, 1536], replicated, may hold values from -0.21875 to 0.21875
Outputs:
- block_output: bfloat16 [2, 8192, 1536], P('batch', 'seq')
- input_grad: bfloat16 [2, 8192, 1536], P('batch', 'seq')
- gain_input_grad: float32 [1536], replicated
- gain_middle_grad: float32 [768], replicated
Inputs may be any that keep to these rules, and one draw needn't show every extreme that they name: `contig_lengths`: row w lists in order the lengths of the 4 contigs packed into window w; they sum to 8192.
All inputs are finite; a program needn't handle non-finite values.
Results may differ from a plain program's by a relative error of at most 0.0065.
Values may be sent and summed in bfloat16 or wider, within the bound.
No kernel may reach another device: no remote copies, remote signals or barrier semaphores. Data moves between devices by JAX's collectives and lax.ppermute only.
A program may use at most 64 MiB of HBM per device.

v0:
```python
import math
import jax
import jax.numpy as jnp
from jax import lax
from jax.sharding import PartitionSpec as P

SPAN = 2
epsilon = 1e-06


def shifted(x, axis, by):
    peers = lax.axis_size(axis)
    pairs = [(i, i + by) for i in range(peers) if 0 <= i + by < peers]
    return lax.ppermute(x, axis, pairs)


def norm_activate(values, scales):
    mean_square = jnp.mean(values * values, axis=-1, keepdims=True)
    return jax.nn.gelu(values * lax.rsqrt(mean_square + epsilon) * scales, approximate=True)


def contig_owner(lengths, positions):
    bounds = jnp.cumsum(lengths)
    return jnp.sum((positions[:, None] >= bounds[None, :]).astype(jnp.int32), axis=1)


def body(
    activations, cotangent, contig_lengths, gain_input, tap_weights, gain_middle, point_weights
):
    signal = activations[0]
    upstream = cotangent[0]
    lengths = contig_lengths[0]
    shard_rows = signal.shape[0]
    seq_count = lax.axis_size("seq")
    tap_reach = SPAN * shard_rows
    total_length = shard_rows * seq_count
    positions = lax.axis_index("seq") * shard_rows + jnp.arange(shard_rows, dtype=jnp.int32)
    owners = contig_owner(lengths, positions)
    before_valid = (
        (positions >= tap_reach) & (contig_owner(lengths, positions - tap_reach) == owners)
    ).astype(jnp.float32)[:, None]
    after_valid = (
        (positions < total_length - tap_reach)
        & (contig_owner(lengths, positions + tap_reach) == owners)
    ).astype(jnp.float32)[:, None]
    tap_before = tap_weights[0]
    tap_center = tap_weights[1]
    tap_after = tap_weights[2]
    normed, input_vjp = jax.vjp(norm_activate, signal.astype(jnp.float32), gain_input)
    hidden = normed.astype(jnp.bfloat16)
    hidden_before = shifted(hidden, "seq", SPAN)
    hidden_after = shifted(hidden, "seq", -SPAN)
    combined = jnp.dot(hidden, tap_center, preferred_element_type=jnp.float32)
    combined = combined + before_valid * jnp.dot(
        hidden_before, tap_before, preferred_element_type=jnp.float32
    )
    combined = combined + after_valid * jnp.dot(
        hidden_after, tap_after, preferred_element_type=jnp.float32
    )
    middle_f, middle_vjp = jax.vjp(norm_activate, combined, gain_middle)
    middle = middle_f.astype(jnp.bfloat16)
    output = (
        signal.astype(jnp.float32)
        + jnp.dot(middle, point_weights, preferred_element_type=jnp.float32)
    ).astype(jnp.bfloat16)
    grad_middle = jnp.dot(upstream, point_weights.T, preferred_element_type=jnp.float32)
    grad_combined_f, middle_terms = middle_vjp(grad_middle)
    grad_combined = grad_combined_f.astype(jnp.bfloat16)
    grad_hidden = jnp.dot(grad_combined, tap_center.T, preferred_element_type=jnp.float32)
    forward_terms = jnp.dot(grad_combined, tap_after.T, preferred_element_type=jnp.float32)
    backward_terms = jnp.dot(grad_combined, tap_before.T, preferred_element_type=jnp.float32)
    terms_before = shifted(forward_terms.astype(jnp.bfloat16), "seq", SPAN).astype(
        forward_terms.dtype
    )
    terms_after = shifted(backward_terms.astype(jnp.bfloat16), "seq", -SPAN).astype(
        backward_terms.dtype
    )
    grad_hidden = grad_hidden + before_valid * terms_before + after_valid * terms_after
    grad_signal, input_terms = input_vjp(grad_hidden)
    grad_output = (upstream.astype(jnp.float32) + grad_signal).astype(jnp.bfloat16)
    summed = lax.psum((input_terms, middle_terms), ("seq", "batch"))
    factor = 1.0 / math.sqrt(lax.axis_size("batch") * seq_count * shard_rows)
    return (output[None], grad_output[None], summed[0] * factor, summed[1] * factor)


def solution(mesh):
    placed = (
        P("batch", "seq", None),
        P("batch", "seq", None),
        P("batch", None),
        P(),
        P(),
        P(),
        P(),
    )
    return jax.shard_map(
        body,
        mesh=mesh,
        in_specs=placed,
        out_specs=(P("batch", "seq", None), P("batch", "seq", None), P(), P()),
        check_vma=False,
    )
```

profile of v0, /device:TPU:0, one launch (start us, length us, event | category | flops | bytes accessed | tf_op | source)
XLA Modules:
  0.0 216.5 jit_solution(4614288820705404492)
XLA Ops:
  0.6 0.0 copy-start
  0.6 0.0 copy-start.1
  0.7 0.0 copy-start.4
  0.7 1.9 fusion.16
  2.6 0.1 copy-done.1
  2.7 3.2 %fusion.12 = bf16[512,1536]{1,0:T(8,128)(2,1)} fusion(bf16[1,512,1536]{2,1,0:T(8,128)(2,1)S(1)} %copy-done.1, f32[1536]{0:T(1024)} %param.10, f32[512]{0:T(512)S(1)} %fusion.88), kind=kLoop, calls=%fused_computation.18 | loop fusion | flops 9437184 | bytes 3153920 | tf_op jit(solution)/shard_map/convert_element_type | solution.py:50
  5.9 6.0 %collective-permute-start = (bf16[512,1536]{1,0:T(8,128)(2,1)}, bf16[512,1536]{1,0:T(8,128)(2,1)}, u32[]{:S(2)}, u32[]{:S(2)}) collective-permute-start(bf16[512,1536]{1,0:T(8,128)(2,1)} %fusion.12), channel_id=1, source_target_pairs={{0,4},{2,6},{4,8},{6,10},{8,12},{10,14},{12,16},{14,18},{16,20},{1... | collective-permute-start | bytes 4718600 | tf_op jit(solution)/shard_map/ppermute | solution.py:14
  11.9 1.3 collective-permute-start.1
  13.2 0.2 reduce-window.8
  13.4 0.1 convert_reduce_fusion.2
  13.5 4.4 %fusion.42 = f32[512,768]{1,0:T(8,128)S(1)} fusion(bf16[3,1536,768]{2,1,0:T(8,128)(2,1)} %param.11, bf16[1,512,1536]{2,1,0:T(8,128)(2,1)} %param.7, f32[1536]{0:T(1024)S(1)} %copy-done.4, f32[512]{0:T(512)S(1)} %fusion.88), kind=kOutput, calls=%fused_computation.51 | convolution fusion | flops 1217396736 | bytes 5513216 | tf_op jit(solution)/shard_map/dot_general | solution.py:53
  17.9 60.5 %collective-permute-done = bf16[512,1536]{1,0:T(8,128)(2,1)} collective-permute-done((bf16[512,1536]{1,0:T(8,128)(2,1)}, bf16[512,1536]{1,0:T(8,128)(2,1)}, u32[]{:S(2)}, u32[]{:S(2)}) %collective-permute-start) | collective-permute-done | bytes 1572896 | tf_op jit(solution)/shard_map/ppermute | solution.py:14
  78.4 3.5 %fusion.38 = f32[512,768]{1,0:T(8,128)S(1)} fusion(bf16[512,1536]{1,0:T(8,128)(2,1)} %collective-permute-done, bf16[3,1536,768]{2,1,0:T(8,128)(2,1)} %param.11), kind=kOutput, calls=%fused_computation.47 | convolution fusion | flops 1207959552 | bytes 5505024 | tf_op jit(solution)/shard_map/dot_general | solution.py:54
  81.9 0.0 copy-start.3
  82.0 0.0 copy-start.5
  82.0 3.8 %multiply_reduce_fusion.2 = (f32[512]{0:T(512)S(1)}, f32[512,768]{1,0:T(8,128)S(1)}) fusion(bf16[512,1536]{1,0:T(8,128)(2,1)} %collective-permute-done.1, bf16[3,1536,768]{2,1,0:T(8,128)(2,1)} %param.11, f32[512]{0:T(512)S(1)} %get-tuple-element.14, f32[512,768]{1,0:T(8,128)S(1)} %fusion.42, f32[512,768]{1,0:T(8,128)S(1)} %fusion.38, ...), kind=kOutput, calls=%fused_computation.75 | convolution fusion | flops 1210318336 | bytes 8656896 | tf_op jit(solution)/shard_map/dot_general | solution.py:57
  85.8 0.0 slice-start
  85.9 2.5 %multiply_reduce_fusion = (f32[768]{0:T(1024)S(1)}, f32[512]{0:T(512)S(1)}, f32[512,768]{1,0:T(8,128)S(1)}) fusion(f32[512,768]{1,0:T(8,128)S(1)} %get-tuple-element.16, f32[512]{0:T(512)S(1)} %fusion.89, f32[768]{0:T(1024)S(1)} %copy-done.5, bf16[768,1536]{1,0:T(8,128)(2,1)S(1)} %copy-done, bf16[1,512,1536]{2,1,0:T(8,128)(2,1)S(1)} %copy-done.3), kind=kOutput, calls=%fused_computation.72 | convolution fusion | flops 1218181888 | bytes 7088128 | tf_op jit(solution)/shard_map/dot_general | solution.py:66
  88.4 0.4 fusion.58
  88.8 0.1 slice-done.1
  88.9 1.4 convolution_convert_fusion
  90.3 0.0 copy-start.2
  90.4 1.4 convolution_convert_fusion.1
  91.8 4.5 %collective-permute-start.2 = (bf16[512,1536]{1,0:T(8,128)(2,1)S(1)}, bf16[512,1536]{1,0:T(8,128)(2,1)S(1)}, u32[]{:S(2)}, u32[]{:S(2)}) collective-permute-start(bf16[512,1536]{1,0:T(8,128)(2,1)S(1)} %convolution_convert_fusion.1), channel_id=1, source_target_pairs={{0,4},{2,6},{4,8},{6,10},{8,12},{10,14},{12,16},{14,18},{16,20},{1... | collective-permute-start | bytes 4718600 | tf_op jit(solution)/shard_map/ppermute | solution.py:14
  96.3 1.5 collective-permute-start.3
  97.8 2.8 %fusion.33 = bf16[1,512,1536]{2,1,0:T(8,128)(2,1)} fusion(bf16[768,1536]{1,0:T(8,128)(2,1)S(1)} %copy-done, bf16[1,512,1536]{2,1,0:T(8,128)(2,1)S(1)} %copy-done.2, f32[512,768]{1,0:T(8,128)S(1)} %get-tuple-element.16, f32[768]{0:T(1024)S(1)} %copy-done.5, f32[512]{0:T(512)S(1)} %fusion.89), kind=kOutput, calls=%fused_computation.41 | convolution fusion | flops 1214644224 | bytes 7083008 | tf_op jit(solution)/shard_map/dot_general | solution.py:64
  100.6 62.0 %collective-permute-done.2 = bf16[512,1536]{1,0:T(8,128)(2,1)S(1)} collective-permute-done((bf16[512,1536]{1,0:T(8,128)(2,1)S(1)}, bf16[512,1536]{1,0:T(8,128)(2,1)S(1)}, u32[]{:S(2)}, u32[]{:S(2)}) %collective-permute-start.2) | collective-permute-done | bytes 1572896 | tf_op jit(solution)/shard_map/ppermute | solution.py:14
  162.7 6.1 %fusion.15 = (f32[1536]{0:T(1024)S(1)}, f32[512]{0:T(512)S(1)}, f32[512,1536]{1,0:T(8,128)}) fusion(bf16[1,512,1536]{2,1,0:T(8,128)(2,1)S(1)} %copy-done.2, f32[512]{0:T(512)S(1)} %fusion.88, f32[1536]{0:T(1024)S(1)} %copy-done.4, bf16[512,1536]{1,0:T(8,128)(2,1)S(1)} %collective-permute-done.3, f32[512]{0:T(512)S(1)} %get-tuple-element.14, ...), kind=kOutput, calls=%fused_computation.21 | convolution fusion | flops 1233909760 | bytes 11032576 | tf_op jit(solution)/shard_map/dot_general | solution.py:69
  168.8 41.6 %all-reduce = (f32[1536]{0:T(1024)S(1)}, f32[768]{0:T(1024)S(1)}) all-reduce(f32[1536]{0:T(1024)S(1)} %get-tuple-element.4, f32[768]{0:T(1024)S(1)} %get-tuple-element.6), channel_id=1, replica_groups=mesh['seq'=16,'batch'=2] {'seq','batch'}, use_global_device_ids=true, to_apply=%region_9.10 | all-reduce | flops 2304 | bytes 18432 | tf_op jit(solution)/shard_map/psum | solution.py:81
  210.4 0.6 broadcast_multiply_fusion
  211.0 0.6 broadcast_multiply_fusion.1
  211.6 4.9 %fusion.59 = bf16[1,512,1536]{2,1,0:T(8,128)(2,1)} fusion(bf16[1,512,1536]{2,1,0:T(8,128)(2,1)} %param.7, f32[512,1536]{1,0:T(8,128)} %get-tuple-element.18, bf16[1,512,1536]{2,1,0:T(8,128)(2,1)} %param.8, f32[512]{0:T(512)S(1)} %multiply_multiply_fusion.6, f32[1536]{0:T(1024)S(1)} %copy-done.4, f32[512]{0:T(512)S(1)} %fusion.88), kind=kLoop, calls=%fused_computation.68 | loop fusion | flops 7077888 | bytes 7874560 | tf_op jit(solution)/shard_map/broadcast_in_dim | solution.py:83
  (19 shorter events, 0.1 us)
Async XLA Ops:
  0.6 85.2 %copy-start = (bf16[768,1536]{1,0:T(8,128)(2,1)S(1)}, bf16[768,1536]{1,0:T(8,128)(2,1)}, u32[]{:S(2)}) copy-start(bf16[768,1536]{1,0:T(8,128)(2,1)} %param.13) | copy-start | bytes 7077892
  0.6 2.0 copy-start.1
  0.7 12.8 %copy-start.4 = (f32[1536]{0:T(1024)S(1)}, f32[1536]{0:T(1024)}, u32[]{:S(2)}) copy-start(f32[1536]{0:T(1024)} %param.10) | copy-start | bytes 18436
  0.7 12.5 %copy-start.6 = (s32[1,4]{1,0:T(1,128)S(1)}, s32[1,4]{1,0:T(1,128)}, u32[]{:S(2)}) copy-start(s32[1,4]{1,0:T(1,128)} %param.9) | copy-start | bytes 52
  5.9 72.5 %collective-permute-start = (bf16[512,1536]{1,0:T(8,128)(2,1)}, bf16[512,1536]{1,0:T(8,128)(2,1)}, u32[]{:S(2)}, u32[]{:S(2)}) collective-permute-start(bf16[512,1536]{1,0:T(8,128)(2,1)} %fusion.12), channel_id=1, source_target_pairs={{0,4},{2,6},{4,8},{6,10},{8,12},{10,14},{12,16},{14,18},{16,20},{1... | collective-permute-start | bytes 4718600 | tf_op jit(solution)/shard_map/ppermute | solution.py:14
  11.9 70.0 %collective-permute-start.1 = (bf16[512,1536]{1,0:T(8,128)(2,1)}, bf16[512,1536]{1,0:T(8,128)(2,1)}, u32[]{:S(2)}, u32[]{:S(2)}) collective-permute-start(bf16[512,1536]{1,0:T(8,128)(2,1)} %fusion.12), channel_id=1, source_target_pairs={{4,0},{6,2},{8,4},{10,6},{12,8},{14,10},{16,12},{18,14},{20,16},{2... | collective-permute-start | bytes 4718600 | tf_op jit(solution)/shard_map/ppermute | solution.py:14
  81.9 3.9 %copy-start.3 = (bf16[1,512,1536]{2,1,0:T(8,128)(2,1)S(1)}, bf16[1,512,1536]{2,1,0:T(8,128)(2,1)}, u32[]{:S(2)}) copy-start(bf16[1,512,1536]{2,1,0:T(8,128)(2,1)} %param.8) | copy-start | bytes 4718596
  82.0 3.9 %copy-start.5 = (f32[768]{0:T(1024)S(1)}, f32[768]{0:T(1024)}, u32[]{:S(2)}) copy-start(f32[768]{0:T(1024)} %param.12) | copy-start | bytes 9220
  85.8 3.0 %slice-start = ((s8[7077888]{0:T(1024)(128)(4,1)}), s8[4194304]{0:T(1024)(128)(4,1)S(1)}, s32[]{:S(2)}) async-start(s8[7077888]{0:T(1024)(128)(4,1)} %bitcast.116), calls=%async_computation | async-start | bytes 8388608
  85.9 3.1 %slice-start.1 = ((s8[7077888]{0:T(1024)(128)(4,1)}), s8[2883584]{0:T(1024)(128)(4,1)S(1)}, s32[]{:S(2)}) async-start(s8[7077888]{0:T(1024)(128)(4,1)} %bitcast.116), calls=%async_computation.1 | async-start | bytes 5767168
  90.3 7.4 %copy-start.2 = (bf16[1,512,1536]{2,1,0:T(8,128)(2,1)S(1)}, bf16[1,512,1536]{2,1,0:T(8,128)(2,1)}, u32[]{:S(2)}) copy-start(bf16[1,512,1536]{2,1,0:T(8,128)(2,1)} %param.7) | copy-start | bytes 4718596
  91.8 70.9 %collective-permute-start.2 = (bf16[512,1536]{1,0:T(8,128)(2,1)S(1)}, bf16[512,1536]{1,0:T(8,128)(2,1)S(1)}, u32[]{:S(2)}, u32[]{:S(2)}) collective-permute-start(bf16[512,1536]{1,0:T(8,128)(2,1)S(1)} %convolution_convert_fusion.1), channel_id=1, source_target_pairs={{0,4},{2,6},{4,8},{6,10},{8,12},{10,14},{12,16},{14,18},{16,20},{1... | collective-permute-start | bytes 4718600 | tf_op jit(solution)/shard_map/ppermute | solution.py:14
  96.3 66.4 %collective-permute-start.3 = (bf16[512,1536]{1,0:T(8,128)(2,1)S(1)}, bf16[512,1536]{1,0:T(8,128)(2,1)S(1)}, u32[]{:S(2)}, u32[]{:S(2)}) collective-permute-start(bf16[512,1536]{1,0:T(8,128)(2,1)S(1)} %convolution_convert_fusion), channel_id=1, source_target_pairs={{4,0},{6,2},{8,4},{10,6},{12,8},{14,10},{16,12},{18,14},{20,16},{2... | collective-permute-start | bytes 4718600 | tf_op jit(solution)/shard_map/ppermute | solution.py:14
where the time goes:
time: 217 us
  waiting for transfers between devices  123 us (57%)
  blocking collectives  41.6 us (19%)
  matrix products  26.1 us (12%)
  starting transfers between devices  13.2 us (6%)
  other arithmetic  11.9 us (5%)
    ppermute x4, waiting for transfers between devices, shifted(): return lax.ppermute(x, axis, pairs)  123 us
    psum x1, blocking collectives, body(): summed = lax.psum((input_terms, middle_terms), ('seq', 'batch'))  41.6 us
    ppermute x4, starting transfers between devices, shifted(): return lax.ppermute(x, axis, pairs)  13.2 us
    dot_general x1, matrix products, body(): jnp.dot(grad_combined, tap_center.T, preferred_element_type=jnp.float32)  6.12 us
    broadcast_in_dim x1, other arithmetic, body(): grad_output[None]  4.9 us
    dot_general x1, matrix products, body(): combined = jnp.dot(hidden, tap_center, preferred_element_type=jnp.float32)  4.44 us
  transfers between devices with their start and end apart: 4, of which 2 were waited for; matrix products, arithmetic and copies ran while one was open for 5% of the time, Pallas kernels for 0%

commit v1 on v0

--- a/solution.py
+++ b/solution.py
@@ -6,6 +6,11 @@
 
 SPAN = 2
 epsilon = 1e-06
+
+
+def by_each_axis(value, axis_one, axis_two):
+    half = lax.psum(value, axis_one)
+    return lax.psum(half, axis_two)
 
 
 def shifted(x, axis, by):
@@ -78,7 +83,7 @@
     grad_hidden = grad_hidden + before_valid * terms_before + after_valid * terms_after
     grad_signal, input_terms = input_vjp(grad_hidden)
     grad_output = (upstream.astype(jnp.float32) + grad_signal).astype(jnp.bfloat16)
-    summed = lax.psum((input_terms, middle_terms), ("seq", "batch"))
+    summed = by_each_axis((input_terms, middle_terms), "batch", "seq")
     factor = 1.0 / math.sqrt(lax.axis_size("batch") * seq_count * shard_rows)
     return (output[None], grad_output[None], summed[0] * factor, summed[1] * factor)
 

time: 217 us -> 242 us (1.12)
  blocking collectives: 41.6 us -> 66.4 us
    psum x1 -> x2, blocking collectives: 41.6 us -> 66.4 us  [the longest x1 58.3 us: by_each_axis(): return lax.psum(half, axis_two)]
where the time goes in v1:
time: 242 us; the launch traced here: 241 us
  waiting for transfers between devices  123 us (51%)
  blocking collectives  66.4 us (27%)
  matrix products  26.1 us (11%)
  starting transfers between devices  13.2 us (5%)
  other arithmetic  11.9 us (5%)
    ppermute x4, waiting for transfers between devices, shifted(): return lax.ppermute(x, axis, pairs)  123 us
    psum x1, blocking collectives, by_each_axis(): return lax.psum(half, axis_two)  58.3 us
    ppermute x4, starting transfers between devices, shifted(): return lax.ppermute(x, axis, pairs)  13.2 us
    psum x1, blocking collectives, by_each_axis(): half = lax.psum(value, axis_one)  8.11 us
    dot_general x1, matrix products, body(): jnp.dot(grad_combined, tap_center.T, preferred_element_type=jnp.float32)  6.12 us
    broadcast_in_dim x1, other arithmetic, body(): grad_output[None]  4.9 us
  transfers between devices with their start and end apart: 4, of which 2 were waited for; matrix products, arithmetic and copies ran while one was open for 5% of the time, Pallas kernels for 0%

profile of v1, /device:TPU:0, one launch (start us, length us, event | category | flops | bytes accessed | tf_op | source)
XLA Modules:
  0.0 241.3 jit_solution(3740659526648683788)
XLA Ops:
  0.6 0.0 copy-start
  0.6 0.0 copy-start.1
  0.7 0.0 copy-start.4
  0.7 1.9 fusion.16
  2.6 0.1 copy-done.1
  2.7 3.2 %fusion.12 = bf16[512,1536]{1,0:T(8,128)(2,1)} fusion(bf16[1,512,1536]{2,1,0:T(8,128)(2,1)S(1)} %copy-done.1, f32[1536]{0:T(1024)} %param.10, f32[512]{0:T(512)S(1)} %fusion.88), kind=kLoop, calls=%fused_computation.18 | loop fusion | flops 9437184 | bytes 3153920 | tf_op jit(solution)/shard_map/convert_element_type | solution.py:55
  5.9 6.0 %collective-permute-start = (bf16[512,1536]{1,0:T(8,128)(2,1)}, bf16[512,1536]{1,0:T(8,128)(2,1)}, u32[]{:S(2)}, u32[]{:S(2)}) collective-permute-start(bf16[512,1536]{1,0:T(8,128)(2,1)} %fusion.12), channel_id=1, source_target_pairs={{0,4},{2,6},{4,8},{6,10},{8,12},{10,14},{12,16},{14,18},{16,20},{1... | collective-permute-start | bytes 4718600 | tf_op jit(solution)/shard_map/ppermute | solution.py:19
  11.9 1.3 collective-permute-start.1
  13.2 0.2 reduce-window.8
  13.4 0.1 convert_reduce_fusion.2
  13.5 4.4 %fusion.42 = f32[512,768]{1,0:T(8,128)S(1)} fusion(bf16[3,1536,768]{2,1,0:T(8,128)(2,1)} %param.11, bf16[1,512,1536]{2,1,0:T(8,128)(2,1)} %param.7, f32[1536]{0:T(1024)S(1)} %copy-done.4, f32[512]{0:T(512)S(1)} %fusion.88), kind=kOutput, calls=%fused_computation.51 | convolution fusion | flops 1217396736 | bytes 5513216 | tf_op jit(solution)/shard_map/dot_general | solution.py:58
  17.9 60.5 %collective-permute-done = bf16[512,1536]{1,0:T(8,128)(2,1)} collective-permute-done((bf16[512,1536]{1,0:T(8,128)(2,1)}, bf16[512,1536]{1,0:T(8,128)(2,1)}, u32[]{:S(2)}, u32[]{:S(2)}) %collective-permute-start) | collective-permute-done | bytes 1572896 | tf_op jit(solution)/shard_map/ppermute | solution.py:19
  78.4 3.5 %fusion.38 = f32[512,768]{1,0:T(8,128)S(1)} fusion(bf16[512,1536]{1,0:T(8,128)(2,1)} %collective-permute-done, bf16[3,1536,768]{2,1,0:T(8,128)(2,1)} %param.11), kind=kOutput, calls=%fused_computation.47 | convolution fusion | flops 1207959552 | bytes 5505024 | tf_op jit(solution)/shard_map/dot_general | solution.py:59
  81.9 0.0 copy-start.3
  82.0 0.0 copy-start.5
  82.0 3.8 %multiply_reduce_fusion.2 = (f32[512]{0:T(512)S(1)}, f32[512,768]{1,0:T(8,128)S(1)}) fusion(bf16[512,1536]{1,0:T(8,128)(2,1)} %collective-permute-done.1, bf16[3,1536,768]{2,1,0:T(8,128)(2,1)} %param.11, f32[512]{0:T(512)S(1)} %get-tuple-element.16, f32[512,768]{1,0:T(8,128)S(1)} %fusion.42, f32[512,768]{1,0:T(8,128)S(1)} %fusion.38, ...), kind=kOutput, calls=%fused_computation.75 | convolution fusion | flops 1210318336 | bytes 8656896 | tf_op jit(solution)/shard_map/dot_general | solution.py:62
  85.8 0.0 slice-start
  85.9 2.5 %multiply_reduce_fusion = (f32[768]{0:T(1024)S(1)}, f32[512]{0:T(512)S(1)}, f32[512,768]{1,0:T(8,128)S(1)}) fusion(f32[512,768]{1,0:T(8,128)S(1)} %get-tuple-element.18, f32[512]{0:T(512)S(1)} %fusion.89, f32[768]{0:T(1024)S(1)} %copy-done.5, bf16[768,1536]{1,0:T(8,128)(2,1)S(1)} %copy-done, bf16[1,512,1536]{2,1,0:T(8,128)(2,1)S(1)} %copy-done.3), kind=kOutput, calls=%fused_computation.72 | convolution fusion | flops 1218181888 | bytes 7088128 | tf_op jit(solution)/shard_map/dot_general | solution.py:71
  88.4 0.4 fusion.58
  88.8 0.1 slice-done.1
  88.9 1.4 convolution_convert_fusion
  90.4 1.4 convolution_convert_fusion.1
  91.8 4.5 %collective-permute-start.2 = (bf16[512,1536]{1,0:T(8,128)(2,1)S(1)}, bf16[512,1536]{1,0:T(8,128)(2,1)S(1)}, u32[]{:S(2)}, u32[]{:S(2)}) collective-permute-start(bf16[512,1536]{1,0:T(8,128)(2,1)S(1)} %convolution_convert_fusion.1), channel_id=1, source_target_pairs={{0,4},{2,6},{4,8},{6,10},{8,12},{10,14},{12,16},{14,18},{16,20},{1... | collective-permute-start | bytes 4718600 | tf_op jit(solution)/shard_map/ppermute | solution.py:19
  96.3 1.5 collective-permute-start.3
  97.8 2.8 %fusion.33 = bf16[1,512,1536]{2,1,0:T(8,128)(2,1)} fusion(bf16[768,1536]{1,0:T(8,128)(2,1)S(1)} %copy-done, bf16[1,512,1536]{2,1,0:T(8,128)(2,1)S(1)} %copy-done.2, f32[512,768]{1,0:T(8,128)S(1)} %get-tuple-element.18, f32[768]{0:T(1024)S(1)} %copy-done.5, f32[512]{0:T(512)S(1)} %fusion.89), kind=kOutput, calls=%fused_computation.41 | convolution fusion | flops 1214644224 | bytes 7083008 | tf_op jit(solution)/shard_map/dot_general | solution.py:69
  100.6 62.0 %collective-permute-done.2 = bf16[512,1536]{1,0:T(8,128)(2,1)S(1)} collective-permute-done((bf16[512,1536]{1,0:T(8,128)(2,1)S(1)}, bf16[512,1536]{1,0:T(8,128)(2,1)S(1)}, u32[]{:S(2)}, u32[]{:S(2)}) %collective-permute-start.2) | collective-permute-done | bytes 1572896 | tf_op jit(solution)/shard_map/ppermute | solution.py:19
  162.7 6.1 %fusion.15 = (f32[1536]{0:T(1024)S(1)}, f32[512]{0:T(512)S(1)}, f32[512,1536]{1,0:T(8,128)}) fusion(bf16[1,512,1536]{2,1,0:T(8,128)(2,1)S(1)} %copy-done.2, f32[512]{0:T(512)S(1)} %fusion.88, f32[1536]{0:T(1024)S(1)} %copy-done.4, bf16[512,1536]{1,0:T(8,128)(2,1)S(1)} %collective-permute-done.3, f32[512]{0:T(512)S(1)} %get-tuple-element.16, ...), kind=kOutput, calls=%fused_computation.21 | convolution fusion | flops 1233909760 | bytes 11032576 | tf_op jit(solution)/shard_map/dot_general | solution.py:74
  168.8 8.1 %all-reduce.1 = (f32[1536]{0:T(1024)S(1)}, f32[768]{0:T(1024)S(1)}) all-reduce(f32[1536]{0:T(1024)S(1)} %get-tuple-element.4, f32[768]{0:T(1024)S(1)} %get-tuple-element.6), channel_id=1, replica_groups=mesh['seq'=16,'batch'=2] {'batch'}, use_global_device_ids=true, to_apply=%region_9.10 | all-reduce | flops 2304 | bytes 18432 | tf_op jit(solution)/shard_map/psum | solution.py:12
  176.9 58.3 %all-reduce = (f32[1536]{0:T(1024)S(1)}, f32[768]{0:T(1024)S(1)}) all-reduce(f32[1536]{0:T(1024)S(1)} %get-tuple-element.13, f32[768]{0:T(1024)S(1)} %get-tuple-element.14), channel_id=1, replica_groups=mesh['seq'=16,'batch'=2] {'seq'}, use_global_device_ids=true, to_apply=%region_10.11 | all-reduce | flops 2304 | bytes 18432 | tf_op jit(solution)/shard_map/psum | solution.py:13
  235.2 0.6 broadcast_multiply_fusion
  235.8 0.6 broadcast_multiply_fusion.1
  236.4 4.9 %fusion.59 = bf16[1,512,1536]{2,1,0:T(8,128)(2,1)} fusion(bf16[1,512,1536]{2,1,0:T(8,128)(2,1)} %param.7, f32[512,1536]{1,0:T(8,128)} %get-tuple-element.20, bf16[1,512,1536]{2,1,0:T(8,128)(2,1)} %param.8, f32[512]{0:T(512)S(1)} %multiply_multiply_fusion.6, f32[1536]{0:T(1024)S(1)} %copy-done.4, f32[512]{0:T(512)S(1)} %fusion.88), kind=kLoop, calls=%fused_computation.68 | loop fusion | flops 7077888 | bytes 7874560 | tf_op jit(solution)/shard_map/broadcast_in_dim | solution.py:88
  (20 shorter events, 0.1 us)
Async XLA Ops:
  0.6 85.2 %copy-start = (bf16[768,1536]{1,0:T(8,128)(2,1)S(1)}, bf16[768,1536]{1,0:T(8,128)(2,1)}, u32[]{:S(2)}) copy-start(bf16[768,1536]{1,0:T(8,128)(2,1)} %param.13) | copy-start | bytes 7077892
  0.6 2.0 copy-start.1
  0.7 12.8 %copy-start.4 = (f32[1536]{0:T(1024)S(1)}, f32[1536]{0:T(1024)}, u32[]{:S(2)}) copy-start(f32[1536]{0:T(1024)} %param.10) | copy-start | bytes 18436
  0.7 12.5 %copy-start.6 = (s32[1,4]{1,0:T(1,128)S(1)}, s32[1,4]{1,0:T(1,128)}, u32[]{:S(2)}) copy-start(s32[1,4]{1,0:T(1,128)} %param.9) | copy-start | bytes 52
  5.9 72.5 %collective-permute-start = (bf16[512,1536]{1,0:T(8,128)(2,1)}, bf16[512,1536]{1,0:T(8,128)(2,1)}, u32[]{:S(2)}, u32[]{:S(2)}) collective-permute-start(bf16[512,1536]{1,0:T(8,128)(2,1)} %fusion.12), channel_id=1, source_target_pairs={{0,4},{2,6},{4,8},{6,10},{8,12},{10,14},{12,16},{14,18},{16,20},{1... | collective-permute-start | bytes 4718600 | tf_op jit(solution)/shard_map/ppermute | solution.py:19
  11.9 70.0 %collective-permute-start.1 = (bf16[512,1536]{1,0:T(8,128)(2,1)}, bf16[512,1536]{1,0:T(8,128)(2,1)}, u32[]{:S(2)}, u32[]{:S(2)}) collective-permute-start(bf16[512,1536]{1,0:T(8,128)(2,1)} %fusion.12), channel_id=1, source_target_pairs={{4,0},{6,2},{8,4},{10,6},{12,8},{14,10},{16,12},{18,14},{20,16},{2... | collective-permute-start | bytes 4718600 | tf_op jit(solution)/shard_map/ppermute | solution.py:19
  81.9 3.9 %copy-start.3 = (bf16[1,512,1536]{2,1,0:T(8,128)(2,1)S(1)}, bf16[1,512,1536]{2,1,0:T(8,128)(2,1)}, u32[]{:S(2)}) copy-start(bf16[1,512,1536]{2,1,0:T(8,128)(2,1)} %param.8) | copy-start | bytes 4718596
  82.0 3.9 %copy-start.5 = (f32[768]{0:T(1024)S(1)}, f32[768]{0:T(1024)}, u32[]{:S(2)}) copy-start(f32[768]{0:T(1024)} %param.12) | copy-start | bytes 9220
  85.8 3.0 %slice-start = ((s8[7077888]{0:T(1024)(128)(4,1)}), s8[4194304]{0:T(1024)(128)(4,1)S(1)}, s32[]{:S(2)}) async-start(s8[7077888]{0:T(1024)(128)(4,1)} %bitcast.116), calls=%async_computation | async-start | bytes 8388608
  85.9 3.1 %slice-start.1 = ((s8[7077888]{0:T(1024)(128)(4,1)}), s8[2883584]{0:T(1024)(128)(4,1)S(1)}, s32[]{:S(2)}) async-start(s8[7077888]{0:T(1024)(128)(4,1)} %bitcast.116), calls=%async_computation.1 | async-start | bytes 5767168
  90.3 7.4 %copy-start.2 = (bf16[1,512,1536]{2,1,0:T(8,128)(2,1)S(1)}, bf16[1,512,1536]{2,1,0:T(8,128)(2,1)}, u32[]{:S(2)}) copy-start(bf16[1,512,1536]{2,1,0:T(8,128)(2,1)} %param.7) | copy-start | bytes 4718596
  91.8 70.9 %collective-permute-start.2 = (bf16[512,1536]{1,0:T(8,128)(2,1)S(1)}, bf16[512,1536]{1,0:T(8,128)(2,1)S(1)}, u32[]{:S(2)}, u32[]{:S(2)}) collective-permute-start(bf16[512,1536]{1,0:T(8,128)(2,1)S(1)} %convolution_convert_fusion.1), channel_id=1, source_target_pairs={{0,4},{2,6},{4,8},{6,10},{8,12},{10,14},{12,16},{14,18},{16,20},{1... | collective-permute-start | bytes 4718600 | tf_op jit(solution)/shard_map/ppermute | solution.py:19
  96.3 66.4 %collective-permute-start.3 = (bf16[512,1536]{1,0:T(8,128)(2,1)S(1)}, bf16[512,1536]{1,0:T(8,128)(2,1)S(1)}, u32[]{:S(2)}, u32[]{:S(2)}) collective-permute-start(bf16[512,1536]{1,0:T(8,128)(2,1)S(1)} %convolution_convert_fusion), channel_id=1, source_target_pairs={{4,0},{6,2},{8,4},{10,6},{12,8},{14,10},{16,12},{18,14},{20,16},{2... | collective-permute-start | bytes 4718600 | tf_op jit(solution)/shard_map/ppermute | solution.py:19
